TPU v7x, 128 devices: a whole 4x4x4 slice. The times are simulated.
128 devices in a mesh: row: 8 (over z, core), col: 16 (over x, y).
Axes of the slice: x: 4, y: 4, z: 4, core: 2. Of those that a mesh axis runs over, the one named last changes fastest.
Arguments:
- tokens: bfloat16 [4096, 2048], P('col', 'row'), may hold values from -6 to 6
- router: bfloat16 [2048, 32], replicated, may hold values from -0.125 to 0.125
- shared_gate_vector: bfloat16 [2048], replicated, may hold values from -0.125 to 0.125
- shared_gate_weight: bfloat16 [2048, 5632], P('col', 'row'), may hold values from -0.125 to 0.125
- shared_up_weight: bfloat16 [2048, 5632], P('col', 'row'), may hold values from -0.125 to 0.125
- shared_down_weight: bfloat16 [5632, 2048], P('row', 'col'), may hold values from -0.078125 to 0.078125
- routed_gate_weight: bfloat16 [32, 2048, 1408], P('col', None, 'row'), may hold values from -0.125 to 0.125
- routed_up_weight: bfloat16 [32, 2048, 1408], P('col', None, 'row'), may hold values from -0.125 to 0.125
- routed_down_weight: bfloat16 [32, 1408, 2048], P('col', 'row'), may hold values from -0.15625 to 0.15625
- adapter_input_factor: bfloat16 [64, 16, 2048], P(None, None, 'row'), may hold values from -0.125 to 0.125
- adapter_output_factor: bfloat16 [64, 16, 5632], P(None, None, 'row'), may hold values from -0.29882812 to 0.29882812
- routes: int32 [4096, 4], P('col'), may hold values from 0 to 31, all different within a row; in each aligned block of 256 rows (0 to 255, 256 to 511, ...) at most 64 rows name the same one
- lengths: int32 [16, 16], P('col'), may hold values from 1 to 128, 256 in all within a row
- prompt_adapter_index: int32 [16, 16], P('col'), may hold values from 0 to 15
- active_adapter_index: int32 [16], replicated, may hold values from 0 to 63, as said below
Outputs:
- moe_out: float32 [4096, 2048], P('col', 'row')
Inputs may be any that keep to these rules, and one draw needn't show every extreme that they name: `routes`: in each group of 256 consecutive tokens no expert is named by more than 64 tokens, a bound that some block reaches. Each group's 16 lengths sum to 256; the longest is exactly 128. `active_adapter_index`: the 16 entries are distinct.
All inputs are finite; a program needn't handle non-finite values.
Results may differ from a plain program's by a relative error of at most 0.003.
Values may be sent and summed in bfloat16 or wider, within the bound.
No kernel may reach another device: no remote copies, remote signals or barrier semaphores. Data moves between devices by JAX's collectives and lax.ppermute only.
A program may use at most 128 MiB of HBM per device.

v0:
```python
import jax
import jax.numpy as jnp
from jax import lax
from jax.sharding import PartitionSpec as P

ADAPTER_SCALE = 2.0


def on_device(
    tokens,
    router,
    shared_gate_vector,
    shared_gate_weight,
    shared_up_weight,
    shared_down_weight,
    routed_gate_weight,
    routed_up_weight,
    routed_down_weight,
    adapter_input_factor,
    adapter_output_factor,
    routes,
    lengths,
    prompt_adapter_index,
    active_adapter_index,
):
    all_features = lax.all_gather(tokens, "row", axis=1, tiled=True)
    token_count = all_features.shape[0]
    full_width = all_features.shape[1]
    local_width = tokens.shape[1]
    col_count = lax.axis_size("col")
    local_experts = routed_gate_weight.shape[0]
    expert_count = local_experts * col_count
    route_count = routes.shape[1]
    capacity = 2 * token_count * route_count // expert_count
    logits = jnp.dot(all_features, router, preferred_element_type=jnp.float32)
    onehot = routes[:, :, None] == jnp.arange(expert_count, dtype=jnp.int32)[None, None, :]
    picked = jnp.sum(jnp.where(onehot, logits[:, None, :], 0.0), axis=2)
    raw_exp = jnp.exp(picked)
    gate_weights = raw_exp / jnp.sum(raw_exp, axis=1, keepdims=True)
    share = jax.nn.sigmoid(
        jnp.dot(all_features, shared_gate_vector, preferred_element_type=jnp.float32)
    )
    hit_table = jnp.any(onehot, axis=1).astype(jnp.int32)
    running_count = jnp.cumsum(hit_table, axis=0)
    slot_rank = running_count - hit_table
    route_rank = jnp.sum(jnp.where(onehot, slot_rank[:, None, :], 0), axis=2)
    row_index = routes * capacity + route_rank
    request_ends = jnp.cumsum(lengths[0])
    request_count = lengths.shape[1]
    token_position = jnp.arange(token_count, dtype=jnp.int32)
    request_of = jnp.sum(
        (token_position[:, None] >= request_ends[None, :]).astype(jnp.int32), axis=1
    )
    request_match = request_of[:, None] == jnp.arange(request_count, dtype=jnp.int32)[None, :]
    adapter_of = jnp.sum(jnp.where(request_match, prompt_adapter_index[0][None, :], 0), axis=1)
    picked_input_factor = jnp.take(adapter_input_factor, active_adapter_index, axis=0)
    rank_width = picked_input_factor.shape[1]
    reduced_rank_value = picked_input_factor.shape[0] * rank_width
    full_in = lax.all_gather(picked_input_factor, "row", axis=2, tiled=True).reshape(
        reduced_rank_value, full_width
    )
    low_rank = lax.dot_general(
        all_features, full_in, (((1,), (1,)), ((), ())), preferred_element_type=jnp.float32
    )
    owner = jnp.arange(reduced_rank_value, dtype=jnp.int32) // rank_width
    adapter_mask = adapter_of[:, None] == owner[None, :]
    low_masked = jnp.where(adapter_mask, low_rank.astype(jnp.bfloat16), jnp.zeros((), jnp.bfloat16))
    picked_output_factor = jnp.take(adapter_output_factor, active_adapter_index, axis=0).reshape(
        reduced_rank_value, adapter_output_factor.shape[2]
    )
    adapter_update = jnp.dot(low_masked, picked_output_factor, preferred_element_type=jnp.float32)
    shared_gate_value = jnp.dot(
        all_features,
        lax.all_gather(shared_gate_weight, "col", axis=0, tiled=True),
        preferred_element_type=jnp.float32,
    )
    shared_up_value = jnp.dot(
        all_features,
        lax.all_gather(shared_up_weight, "col", axis=0, tiled=True),
        preferred_element_type=jnp.float32,
    )
    shared_hidden_units = (
        jax.nn.silu(shared_gate_value) * (shared_up_value + ADAPTER_SCALE * adapter_update)
    ).astype(jnp.bfloat16)
    shared_part = jnp.dot(
        shared_hidden_units,
        lax.all_gather(shared_down_weight, "col", axis=1, tiled=True),
        preferred_element_type=jnp.float32,
    )
    shared_part = shared_part * share[:, None]
    positions = jnp.arange(capacity, dtype=jnp.int32)
    slot_token = jnp.sum(
        (running_count.T[:, None, :] <= positions[None, :, None]).astype(jnp.int32), axis=2
    )
    slot_valid = positions[None, :] < running_count[-1][:, None]
    picked_rows = jnp.take(all_features, jnp.minimum(slot_token, token_count - 1), axis=0)
    chosen = jnp.where(slot_valid[:, :, None], picked_rows, jnp.zeros((), jnp.bfloat16))
    outgoing = chosen.reshape(col_count, local_experts, capacity, full_width)
    slot_block = lax.all_to_all(outgoing, "col", split_axis=0, concat_axis=0, tiled=True)
    gate_part = jnp.einsum(
        "sexd,edf->sexf", slot_block, routed_gate_weight, preferred_element_type=jnp.float32
    )
    up_part = jnp.einsum(
        "sexd,edf->sexf", slot_block, routed_up_weight, preferred_element_type=jnp.float32
    )
    hidden = (jax.nn.silu(gate_part) * up_part).astype(jnp.bfloat16)
    partial_value = jnp.einsum(
        "sexf,efd->sexd", hidden, routed_down_weight, preferred_element_type=jnp.float32
    )
    summed, shared_sum = (
        lax.psum_scatter(partial_value, "row", scatter_dimension=3, tiled=True),
        lax.psum_scatter(shared_part, "row", scatter_dimension=1, tiled=True),
    )
    returned = lax.all_to_all(summed, "col", split_axis=0, concat_axis=0, tiled=True)
    flat_rows = returned.reshape(expert_count * capacity, local_width)
    routed_rows = jnp.take(flat_rows, row_index, axis=0)
    routed = jnp.sum(gate_weights[:, :, None] * routed_rows, axis=1)
    return routed + shared_sum


def solution(mesh):
    return jax.shard_map(
        on_device,
        mesh=mesh,
        in_specs=(
            P("col", "row"),
            P(),
            P(),
            P("col", "row"),
            P("col", "row"),
            P("row", "col"),
            P("col", None, "row"),
            P("col", None, "row"),
            P("col", "row", None),
            P(None, None, "row"),
            P(None, None, "row"),
            P("col", None),
            P("col", None),
            P("col", None),
            P(),
        ),
        out_specs=P("col", "row"),
        check_vma=False,
    )
```

profile of v0, /device:TPU:0, one launch (start us, length us, event | category | flops | bytes accessed | tf_op | source)
XLA Modules:
  0.0 487.8 jit_solution(12929686134690936716)
XLA Ops:
  6.5 0.7 all-gather.6.cloned.1.call-update
  7.3 0.7 compare_select_fusion.3
  8.0 1.6 gather_fusion.2
  9.6 0.7 compare_and_fusion.2
  10.2 0.7 broadcast_select_fusion
  11.1 0.7 all-gather.8.cloned.1.call-update
  11.8 0.5 all-gather.10.cloned.1.call-update
  12.3 0.7 fusion.29
  13.1 0.6 reduce-window.18
  13.7 0.2 slice_reduce_fusion
  14.0 0.6 convert_reduce_fusion
  14.6 0.2 slice_reduce_fusion.1
  15.0 0.1 compare_and_fusion
  15.1 20.0 %all-gather.6.cloned.1.call-done = bf16[256,2048]{1,0:T(8,128)(2,1)} async-done(((bf16[256,256]{1,0:T(8,128)(2,1)}), bf16[256,2048]{1,0:T(8,128)(2,1)}) %all-gather.6.cloned.1.call-update) | async-done | bytes 1048592 | tf_op jit(solution)/shard_map/all_gather | solution.py:26
  35.0 17.7 %gather_fusion = bf16[2048,2048]{1,0:T(8,128)(2,1)} fusion(bf16[256,2048]{1,0:T(8,128)(2,1)} %all-gather.6.cloned.1.call-done, s32[2048]{0:T(1024)S(1)} %broadcast_clamp_fusion), kind=kCustom, calls=%fused_computation | custom fusion | bytes 16785408 | tf_op jit(solution)/shard_map/jit(_take)/gather | solution.py:96
  52.7 7.5 %select_select_fusion = bf16[16,2,64,2048]{3,2,1,0:T(8,128)(2,1)} fusion(bf16[16,2,64,2048]{3,2,1,0:T(8,128)(2,1)} %bitcast.88, pred[16,2,64]{2,1,0:T(4,128)(4,1)S(1)} %get-tuple-element.9, pred[16,2,64]{2,1,0:T(4,128)(4,1)S(1)} %get-tuple-element.10), kind=kLoop, calls=%fused_computation.4 | loop fusion | flops 8388608 | bytes 16781312 | tf_op jit(solution)/shard_map/jit(_where)/select_n | solution.py:97
  60.2 7.0 %all-to-all-start = ((bf16[16,2,64,2048]{3,2,1,0:T(8,128)(2,1)}), bf16[16,2,64,2048]{3,2,1,0:T(8,128)(2,1)}, u32[]{:S(2)}, u32[]{:S(2)}) async-start(bf16[16,2,64,2048]{3,2,1,0:T(8,128)(2,1)} %select_select_fusion), calls=%async_computation | async-start | bytes 16777216 | tf_op jit(solution)/shard_map/all_to_all | solution.py:99
  67.3 0.5 all-gather.14.cloned.1.call-update
  67.9 152.1 %all-to-all-done = bf16[16,2,64,2048]{3,2,1,0:T(8,128)(2,1)} async-done(((bf16[16,2,64,2048]{3,2,1,0:T(8,128)(2,1)}), bf16[16,2,64,2048]{3,2,1,0:T(8,128)(2,1)}, u32[]{:S(2)}, u32[]{:S(2)}) %all-to-all-start) | async-done | bytes 8388640 | tf_op jit(solution)/shard_map/all_to_all | solution.py:99
  219.9 7.0 %fusion.2 = f32[2,16,64,176]{3,2,1,0:T(8,128)} fusion(bf16[16,2,64,2048]{3,2,1,0:T(8,128)(2,1)} %all-to-all-done, bf16[2,2048,176]{1,2,0:T(8,128)(2,1)S(1)} %copy-done.7), kind=kOutput, calls=%fused_computation.7 | convolution fusion | flops 1476395008 | bytes 11272192 | tf_op jit(solution)/shard_map/sexd,edf->sexf/dot_general | solution.py:100
  227.0 15.2 %convolution_bitcast_fusion = f32[16,2,64,2048]{3,2,0,1:T(8,128)} fusion(f32[2,16,64,176]{3,2,1,0:T(8,128)} %fusion.2, bf16[16,2,64,2048]{3,2,1,0:T(8,128)(2,1)} %all-to-all-done, bf16[2,176,2048]{2,1,0:T(8,128)(2,1)} %param.23, bf16[2,2048,176]{1,2,0:T(8,128)(2,1)} %param.22), kind=kOutput, calls=%fused_computation.9 | convolution fusion | flops 2954952704 | bytes 29491200 | tf_op jit(solution)/shard_map/sexf,efd->sexd/dot_general | solution.py:107
  242.2 0.2 reduce-scatter.5.cloned.1.call-start
  242.5 0.1 broadcast_in_dim.138
  242.6 0.3 copy-done.4
  243.0 0.1 reduce.2
  243.1 0.6 gather_fusion.3
  243.7 0.1 convert_reduce_fusion.1
  243.9 0.1 bitcast_select_fusion
  244.0 0.4 fusion.37
  244.4 1.7 fusion.20
  246.2 3.6 fusion.35
  249.8 35.6 %all-gather.10.cloned.1.call-done = bf16[2048,704]{0,1:T(8,128)(2,1)} async-done(((bf16[128,704]{0,1:T(8,128)(2,1)}), bf16[2048,704]{0,1:T(8,128)(2,1)}) %all-gather.10.cloned.1.call-update) | async-done | bytes 2883600 | tf_op jit(solution)/shard_map/all_gather | solution.py:79
  285.5 3.6 fusion.36
  289.1 48.2 %all-gather.14.cloned.1.call-done = bf16[704,2048]{1,0:T(8,128)(2,1)} async-done(((bf16[704,128]{1,0:T(8,128)(2,1)}), bf16[704,2048]{1,0:T(8,128)(2,1)}) %all-gather.14.cloned.1.call-update) | async-done | bytes 2883600 | tf_op jit(solution)/shard_map/all_gather | solution.py:87
  337.3 4.9 %convolution_multiply_fusion = f32[256,2048]{1,0:T(8,128)} fusion(bf16[704,2048]{1,0:T(8,128)(2,1)} %all-gather.14.cloned.1.call-done, f32[256,704]{0,1:T(8,128)} %fusion.36, bf16[256,256]{0,1:T(8,128)(2,1)S(1)} %fusion.20, bf16[256,704]{1,0:T(8,128)(2,1)S(1)} %bitcast_select_fusion, f32[256]{0:T(256)S(1)} %add_divide_fusion, f32[256,704]{0,1:T(8,128)} %fusion.35), kind=kOutput, calls=%fused_computation.10 | convolution fusion | flops 832438272 | bytes 6915072 | tf_op jit(solution)/shard_map/dot_general | solution.py:85
  342.2 88.8 %reduce-scatter.3.cloned.1.call-done = f32[16,2,64,256]{3,2,0,1:T(8,128)} async-done(((f32[16,2,64,2048]{3,2,0,1:T(8,128)}), f32[16,2,64,256]{3,2,0,1:T(8,128)}) %reduce-scatter.3.cloned.1.call-update) | async-done | bytes 2097168 | tf_op jit(solution)/shard_map/reduce_scatter | solution.py:111
  431.0 3.2 copy.52
  434.2 7.0 %all-to-all-start.1 = ((f32[16,2,64,256]{3,2,1,0:T(8,128)}), f32[16,2,64,256]{3,2,1,0:T(8,128)}, u32[]{:S(2)}, u32[]{:S(2)}) async-start(f32[16,2,64,256]{3,2,1,0:T(8,128)} %copy.52), calls=%async_computation.2 | async-start | bytes 4194304 | tf_op jit(solution)/shard_map/all_to_all | solution.py:114
  441.3 0.2 copy.49
  441.5 0.1 copy.53
  441.7 0.1 reshape.165
  441.8 0.4 fusion.34
  442.3 0.1 copy.46
  442.5 27.9 %all-to-all-done.1 = f32[16,2,64,256]{3,2,1,0:T(8,128)} async-done(((f32[16,2,64,256]{3,2,1,0:T(8,128)}), f32[16,2,64,256]{3,2,1,0:T(8,128)}, u32[]{:S(2)}, u32[]{:S(2)}) %all-to-all-start.1) | async-done | bytes 2097184 | tf_op jit(solution)/shard_map/all_to_all | solution.py:114
  470.3 5.1 %gather_fusion.1 = f32[1024,256]{1,0:T(8,128)S(1)} fusion(f32[2048,256]{1,0:T(8,128)} %bitcast.14, s32[1024]{0:T(1024)S(1)} %broadcast_clamp_fusion.1), kind=kCustom, calls=%fused_computation.1 | custom fusion | bytes 2101248 | tf_op jit(solution)/shard_map/jit(_take)/gather | solution.py:116
  475.4 1.3 reshape.164
  476.7 2.5 multiply_reduce_fusion
  479.2 1.7 add.77
  (51 shorter events, 1.1 us)
Async XLA Ops:
  6.5 236.6 %copy-start = (bf16[64,16,704]{2,1,0:T(8,128)(2,1)S(1)}, bf16[64,16,704]{2,1,0:T(8,128)(2,1)}, u32[]{:S(2)}) copy-start(bf16[64,16,704]{2,1,0:T(8,128)(2,1)} %param.25) | copy-start | bytes 4325380
  6.5 28.5 %all-gather.6.cloned.1.call-start = ((), (), s32[]{:S(2)}) async-start(), calls=%async_computation.4 | async-start | bytes 1179648 | tf_op jit(solution)/shard_map/all_gather | solution.py:26
  7.3 237.2 %all-gather.12.cloned.1.call-start = ((), (), s32[]{:S(2)}) async-start(), calls=%async_computation.8 | async-start | bytes 1179648 | tf_op jit(solution)/shard_map/all_gather | solution.py:59
  11.0 235.2 %all-gather.8.cloned.1.call-start = ((), (), s32[]{:S(2)}) async-start(), calls=%async_computation.6 | async-start | bytes 3063808 | tf_op jit(solution)/shard_map/all_gather | solution.py:74
  11.8 273.7 %all-gather.10.cloned.1.call-start = ((), (), s32[]{:S(2)}) async-start(), calls=%async_computation.7 | async-start | bytes 3063808 | tf_op jit(solution)/shard_map/all_gather | solution.py:79
  60.2 159.7 %copy-start.7 = (bf16[2,2048,176]{1,2,0:T(8,128)(2,1)S(1)}, bf16[2,2048,176]{1,2,0:T(8,128)(2,1)}, u32[]{:S(2)}) copy-start(bf16[2,2048,176]{1,2,0:T(8,128)(2,1)} %param.21) | copy-start | bytes 4325380
  60.2 159.7 %all-to-all-start = ((bf16[16,2,64,2048]{3,2,1,0:T(8,128)(2,1)}), bf16[16,2,64,2048]{3,2,1,0:T(8,128)(2,1)}, u32[]{:S(2)}, u32[]{:S(2)}) async-start(bf16[16,2,64,2048]{3,2,1,0:T(8,128)(2,1)} %select_select_fusion), calls=%async_computation | async-start | bytes 16777216 | tf_op jit(solution)/shard_map/all_to_all | solution.py:99
  67.2 270.1 %all-gather.14.cloned.1.call-start = ((), (), s32[]{:S(2)}) async-start(), calls=%async_computation.9 | async-start | bytes 3063808 | tf_op jit(solution)/shard_map/all_gather | solution.py:87
  67.8 363.2 %reduce-scatter.3.cloned.1.call-start = ((), (), s32[]{:S(2)}) async-start(), calls=%async_computation.5 | async-start | bytes 18874368 | tf_op jit(solution)/shard_map/reduce_scatter | solution.py:111
  242.2 0.7 copy-start.4
  242.2 0.7 copy-start.5
  242.2 1.6 copy-start.6
  242.2 1.8 copy-start.1
  242.2 237.0 %reduce-scatter.5.cloned.1.call-start = ((), (), s32[]{:S(2)}) async-start(), calls=%async_computation.10 | async-start | bytes 2359296 | tf_op jit(solution)/shard_map/reduce_scatter | solution.py:112
  434.2 7.1 %copy-start.3 = (s32[256,4]{0,1:T(4,128)S(1)}, s32[256,4]{0,1:T(4,128)}, u32[]{:S(2)}) copy-start(s32[256,4]{0,1:T(4,128)} %param.26) | copy-start | bytes 12292
  434.2 7.6 %copy-start.2 = (bf16[2048,32]{0,1:T(8,128)(2,1)S(1)}, bf16[2048,32]{0,1:T(8,128)(2,1)}, u32[]{:S(2)}) copy-start(bf16[2048,32]{0,1:T(8,128)(2,1)} %param.16) | copy-start | bytes 393220
  434.2 36.1 %all-to-all-start.1 = ((f32[16,2,64,256]{3,2,1,0:T(8,128)}), f32[16,2,64,256]{3,2,1,0:T(8,128)}, u32[]{:S(2)}, u32[]{:S(2)}) async-start(f32[16,2,64,256]{3,2,1,0:T(8,128)} %copy.52), calls=%async_computation.2 | async-start | bytes 4194304 | tf_op jit(solution)/shard_map/all_to_all | solution.py:114
Sparse Core Ops, SparseCore 0:
  9.0 25.9 all-gather.5
  36.7 24.2 all-gather.11
  63.1 155.2 all-gather.7
  220.5 64.9 all-gather.9
  287.4 49.8 all-gather.13
  339.6 91.3 reduce-scatter.2
  433.4 34.4 reduce-scatter.4
where the time goes:
time: 488 us
  waiting for transfers between devices  375 us (77%)
  matrix products  36.9 us (8%)
  local copies, waits for them, and re-layouts  31 us (6%)
  other arithmetic  16.6 us (3%)
  starting transfers between devices  14.4 us (3%)
  between operations  13.7 us (3%)
    all_to_all x1, waiting for transfers between devices, on_device(): lax.all_to_all(outgoing, 'col', split_axis=0, concat_axis=0, tiled=True)  152 us
    reduce_scatter x1, waiting for transfers between devices, on_device(): lax.psum_scatter(partial_value, 'row', scatter_dimension=3, tiled=True)  88.8 us
    all_gather x1, waiting for transfers between devices, on_device(): lax.all_gather(shared_down_weight, 'col', axis=1, tiled=True)  48.2 us
    all_gather x1, waiting for transfers between devices, on_device(): lax.all_gather(shared_up_weight, 'col', axis=0, tiled=True)  35.6 us
    all_to_all x1, waiting for transfers between devices, on_device(): lax.all_to_all(summed, 'col', split_axis=0, concat_axis=0, tiled=True)  27.9 us
    all_gather x1, waiting for transfers between devices, on_device(): all_features = lax.all_gather(tokens, 'row', axis=1, tiled=True)  20 us
    gather x1, local copies, waits for them, and re-layouts, on_device(): jnp.take(all_features, jnp.minimum(slot_token, token_count - 1), axis=0)  17.7 us
    dot_general x1, matrix products, on_device(): jnp.einsum('sexf,efd->sexd', hidden, routed_down_weight, preferred_elemen...  15.2 us
  transfers between devices with their start and end apart: 9, of which 6 were waited for; matrix products, arithmetic and copies ran while one was open for 17% of the time, Pallas kernels for 0%

commit v1 on v0

--- a/solution.py
+++ b/solution.py
@@ -4,6 +4,13 @@
 from jax.sharding import PartitionSpec as P
 
 ADAPTER_SCALE = 2.0
+
+
+def view_targets(slab_in, row_axis):
+    raw_out = lax.axis_size(row_axis)
+    newest = jnp.stack(raw_out * [slab_in])
+    w1 = lax.all_to_all(newest, row_axis, 0, 0)
+    return jnp.concatenate(w1, axis=1)
 
 
 def on_device(
@@ -23,7 +30,7 @@
     prompt_adapter_index,
     active_adapter_index,
 ):
-    all_features = lax.all_gather(tokens, "row", axis=1, tiled=True)
+    all_features = view_targets(tokens, "row")
     token_count = all_features.shape[0]
     full_width = all_features.shape[1]
     local_width = tokens.shape[1]

time: 488 us -> 452 us (0.926)
  waiting for transfers between devices: 375 us -> 335 us
  starting transfers between devices: 14.4 us -> 19.9 us
    all_gather x1, waiting for transfers between devices: 35.6 us -> 0.02 us  [on_device(): lax.all_gather(shared_up_weight, 'col', axis=0, tiled=True)]
    all_gather x1 -> x0, waiting for transfers between devices: 20 us -> none  [on_device(): all_features = lax.all_gather(tokens, 'row', axis=1, tiled=True)]
    all_to_all x0 -> x1, waiting for transfers between devices: none -> 16.1 us  [view_targets(): w1 = lax.all_to_all(newest, row_axis, 0, 0)]
    all_gather x1, waiting for transfers between devices: 0.02 us -> 8.27 us  [on_device(): lax.all_gather(shared_gate_weight, 'col', axis=0, tiled=True)]
    all_to_all x1, waiting for transfers between devices: 152 us -> 144 us  [on_device(): lax.all_to_all(outgoing, 'col', split_axis=0, concat_axis=0, tiled=True)]
    gather x1, local copies, waits for them, and re-layouts: 17.7 us -> 11 us  [on_device(): jnp.take(all_features, jnp.minimum(slot_token, token_count - 1), axis=0)]
    all_to_all x0 -> x1, starting transfers between devices: none -> 5.43 us  [view_targets(): w1 = lax.all_to_all(newest, row_axis, 0, 0)]
where the time goes in v1:
time: 452 us; the launch traced here: 451 us
  waiting for transfers between devices  335 us (74%)
  matrix products  37.5 us (8%)
  local copies, waits for them, and re-layouts  28.6 us (6%)
  starting transfers between devices  19.9 us (4%)
  other arithmetic  16 us (4%)
  between operations  13.7 us (3%)
    all_to_all x1, waiting for transfers between devices, on_device(): lax.all_to_all(outgoing, 'col', split_axis=0, concat_axis=0, tiled=True)  144 us
    reduce_scatter x1, waiting for transfers between devices, on_device(): lax.psum_scatter(partial_value, 'row', scatter_dimension=3, tiled=True)  88.8 us
    all_gather x1, waiting for transfers between devices, on_device(): lax.all_gather(shared_down_weight, 'col', axis=1, tiled=True)  48.2 us
    all_to_all x1, waiting for transfers between devices, on_device(): lax.all_to_all(summed, 'col', split_axis=0, concat_axis=0, tiled=True)  27.9 us
    all_to_all x1, waiting for transfers between devices, view_targets(): w1 = lax.all_to_all(newest, row_axis, 0, 0)  16.1 us
    dot_general x1, matrix products, on_device(): jnp.einsum('sexf,efd->sexd', hidden, routed_down_weight, preferred_elemen...  15.3 us
    gather x1, local copies, waits for them, and re-layouts, on_device(): jnp.take(all_features, jnp.minimum(slot_token, token_count - 1), axis=0)  11 us
  transfers between devices with their start and end apart: 9, of which 6 were waited for; matrix products, arithmetic and copies ran while one was open for 17% of the time, Pallas kernels for 0%

profile of v1, /device:TPU:0, one launch (start us, length us, event | category | flops | bytes accessed | tf_op | source)
XLA Modules:
  0.0 451.1 jit_solution(3308045273963713759)
XLA Ops:
  6.5 0.8 compare_and_fusion.2
  7.3 0.7 compare_select_fusion.3
  8.0 1.6 gather_fusion.2
  9.6 0.7 broadcast_select_fusion
  10.4 0.7 all-gather.7.cloned.1.call-update
  11.1 1.9 stack.2
  13.1 5.4 %all-to-all-start = ((bf16[8,256,256]{2,1,0:T(8,128)(2,1)}), bf16[8,256,256]{2,1,0:T(8,128)(2,1)S(1)}, u32[]{:S(2)}, u32[]{:S(2)}) async-start(bf16[8,256,256]{2,1,0:T(8,128)(2,1)} %stack.2), calls=%async_computation | async-start | bytes 2097152 | tf_op jit(solution)/shard_map/all_to_all | solution.py:12
  18.5 0.7 all-gather.5.cloned.1.call-update
  19.3 0.6 reduce-window.18
  19.9 0.2 slice_reduce_fusion
  20.2 0.6 convert_reduce_fusion
  20.8 0.2 slice_reduce_fusion.1
  21.3 16.1 %all-to-all-done = bf16[8,256,256]{2,1,0:T(8,128)(2,1)S(1)} async-done(((bf16[8,256,256]{2,1,0:T(8,128)(2,1)}), bf16[8,256,256]{2,1,0:T(8,128)(2,1)S(1)}, u32[]{:S(2)}, u32[]{:S(2)}) %all-to-all-start) | async-done | bytes 1048608 | tf_op jit(solution)/shard_map/all_to_all | solution.py:12
  37.3 1.0 copy-done.1
  38.3 1.3 copy.61
  39.7 11.0 %gather_fusion = bf16[2048,2048]{1,0:T(8,128)(2,1)} fusion(bf16[256,2048]{1,0:T(8,128)(2,1)S(1)} %bitcast.91, s32[2048]{0:T(1024)S(1)} %broadcast_clamp_fusion), kind=kCustom, calls=%fused_computation | custom fusion | bytes 16785408 | tf_op jit(solution)/shard_map/jit(_take)/gather | solution.py:103
  50.7 7.4 %select_select_fusion = bf16[16,2,64,2048]{3,2,1,0:T(8,128)(2,1)} fusion(bf16[16,2,64,2048]{3,2,1,0:T(8,128)(2,1)} %bitcast.97, pred[16,2,64]{2,1,0:T(4,128)(4,1)S(1)} %get-tuple-element.9, pred[16,2,64]{2,1,0:T(4,128)(4,1)S(1)} %get-tuple-element.10), kind=kLoop, calls=%fused_computation.4 | loop fusion | flops 8388608 | bytes 16781312 | tf_op jit(solution)/shard_map/jit(_where)/select_n | solution.py:104
  58.2 7.1 %all-to-all-start.1 = ((bf16[16,2,64,2048]{3,2,1,0:T(8,128)(2,1)}), bf16[16,2,64,2048]{3,2,1,0:T(8,128)(2,1)}, u32[]{:S(2)}, u32[]{:S(2)}) async-start(bf16[16,2,64,2048]{3,2,1,0:T(8,128)(2,1)} %select_select_fusion), calls=%async_computation.1 | async-start | bytes 16777216 | tf_op jit(solution)/shard_map/all_to_all | solution.py:106
  65.3 0.5 all-gather.11.cloned.1.call-update
  65.9 144.2 %all-to-all-done.1 = bf16[16,2,64,2048]{3,2,1,0:T(8,128)(2,1)} async-done(((bf16[16,2,64,2048]{3,2,1,0:T(8,128)(2,1)}), bf16[16,2,64,2048]{3,2,1,0:T(8,128)(2,1)}, u32[]{:S(2)}, u32[]{:S(2)}) %all-to-all-start.1) | async-done | bytes 8388640 | tf_op jit(solution)/shard_map/all_to_all | solution.py:106
  210.1 7.4 %fusion.2 = f32[2,16,64,176]{3,2,1,0:T(8,128)} fusion(bf16[16,2,64,2048]{3,2,1,0:T(8,128)(2,1)} %all-to-all-done.1, bf16[2,2048,176]{1,2,0:T(8,128)(2,1)} %param.21), kind=kOutput, calls=%fused_computation.7 | convolution fusion | flops 1476395008 | bytes 11272192 | tf_op jit(solution)/shard_map/sexd,edf->sexf/dot_general | solution.py:107
  217.5 15.3 %convolution_bitcast_fusion = f32[16,2,64,2048]{3,2,0,1:T(8,128)} fusion(f32[2,16,64,176]{3,2,1,0:T(8,128)} %fusion.2, bf16[16,2,64,2048]{3,2,1,0:T(8,128)(2,1)} %all-to-all-done.1, bf16[2,176,2048]{2,1,0:T(8,128)(2,1)} %param.23, bf16[2,2048,176]{1,2,0:T(8,128)(2,1)} %param.22), kind=kOutput, calls=%fused_computation.9 | convolution fusion | flops 2954952704 | bytes 29491200 | tf_op jit(solution)/shard_map/sexf,efd->sexd/dot_general | solution.py:114
  232.9 0.2 reduce-scatter.5.cloned.1.call-start
  233.2 0.1 broadcast_in_dim.138
  233.2 0.3 copy-done.4
  233.6 0.1 reduce.2
  233.8 0.6 gather_fusion.3
  234.5 0.1 bitcast_select_fusion
  234.6 0.4 fusion.37
  235.1 1.7 fusion.20
  236.8 3.7 fusion.36
  240.5 8.3 %all-gather.5.cloned.1.call-done = bf16[2048,704]{0,1:T(8,128)(2,1)} async-done(((bf16[128,704]{0,1:T(8,128)(2,1)}), bf16[2048,704]{0,1:T(8,128)(2,1)}) %all-gather.5.cloned.1.call-update) | async-done | bytes 2883600 | tf_op jit(solution)/shard_map/all_gather | solution.py:81
  248.8 3.6 fusion.35
  252.4 48.2 %all-gather.11.cloned.1.call-done = bf16[704,2048]{1,0:T(8,128)(2,1)} async-done(((bf16[704,128]{1,0:T(8,128)(2,1)}), bf16[704,2048]{1,0:T(8,128)(2,1)}) %all-gather.11.cloned.1.call-update) | async-done | bytes 2883600 | tf_op jit(solution)/shard_map/all_gather | solution.py:94
  300.7 4.9 %convolution_multiply_fusion = f32[256,2048]{1,0:T(8,128)} fusion(bf16[704,2048]{1,0:T(8,128)(2,1)} %all-gather.11.cloned.1.call-done, f32[256,704]{0,1:T(8,128)} %fusion.36, bf16[256,256]{0,1:T(8,128)(2,1)S(1)} %fusion.20, bf16[256,704]{1,0:T(8,128)(2,1)S(1)} %bitcast_select_fusion, f32[256]{0:T(256)S(1)} %add_divide_fusion, f32[256,704]{0,1:T(8,128)} %fusion.35), kind=kOutput, calls=%fused_computation.10 | convolution fusion | flops 832438272 | bytes 6915072 | tf_op jit(solution)/shard_map/dot_general | solution.py:92
  305.6 88.8 %reduce-scatter.3.cloned.1.call-done = f32[16,2,64,256]{3,2,0,1:T(8,128)} async-done(((f32[16,2,64,2048]{3,2,0,1:T(8,128)}), f32[16,2,64,256]{3,2,0,1:T(8,128)}) %reduce-scatter.3.cloned.1.call-update) | async-done | bytes 2097168 | tf_op jit(solution)/shard_map/reduce_scatter | solution.py:118
  394.4 3.2 copy.54
  397.6 7.0 %all-to-all-start.2 = ((f32[16,2,64,256]{3,2,1,0:T(8,128)}), f32[16,2,64,256]{3,2,1,0:T(8,128)}, u32[]{:S(2)}, u32[]{:S(2)}) async-start(f32[16,2,64,256]{3,2,1,0:T(8,128)} %copy.54), calls=%async_computation.3 | async-start | bytes 4194304 | tf_op jit(solution)/shard_map/all_to_all | solution.py:121
  404.7 0.2 copy.51
  404.9 0.1 copy.55
  405.0 0.1 reshape.175
  405.2 0.4 fusion.34
  405.7 0.1 copy.48
  405.8 27.9 %all-to-all-done.2 = f32[16,2,64,256]{3,2,1,0:T(8,128)} async-done(((f32[16,2,64,256]{3,2,1,0:T(8,128)}), f32[16,2,64,256]{3,2,1,0:T(8,128)}, u32[]{:S(2)}, u32[]{:S(2)}) %all-to-all-start.2) | async-done | bytes 2097184 | tf_op jit(solution)/shard_map/all_to_all | solution.py:121
  433.7 5.1 %gather_fusion.1 = f32[1024,256]{1,0:T(8,128)S(1)} fusion(f32[2048,256]{1,0:T(8,128)} %bitcast.15, s32[1024]{0:T(1024)S(1)} %broadcast_clamp_fusion.1), kind=kCustom, calls=%fused_computation.1 | custom fusion | bytes 2101248 | tf_op jit(solution)/shard_map/jit(_take)/gather | solution.py:123
  438.7 1.3 reshape.174
  440.0 2.5 multiply_reduce_fusion
  442.6 1.7 add.77
  (50 shorter events, 1.3 us)
Async XLA Ops:
  6.5 227.2 %copy-start = (bf16[64,16,704]{2,1,0:T(8,128)(2,1)S(1)}, bf16[64,16,704]{2,1,0:T(8,128)(2,1)}, u32[]{:S(2)}) copy-start(bf16[64,16,704]{2,1,0:T(8,128)(2,1)} %param.25) | copy-start | bytes 4325380
  6.5 228.5 %all-gather.9.cloned.1.call-start = ((), (), s32[]{:S(2)}) async-start(), calls=%async_computation.8 | async-start | bytes 1179648 | tf_op jit(solution)/shard_map/all_gather | solution.py:66
  8.0 11.3 %copy-start.3 = (s32[256,4]{0,1:T(4,128)S(1)}, s32[256,4]{0,1:T(4,128)}, u32[]{:S(2)}) copy-start(s32[256,4]{0,1:T(4,128)} %param.26) | copy-start | bytes 12292
  10.4 226.4 %all-gather.7.cloned.1.call-start = ((), (), s32[]{:S(2)}) async-start(), calls=%async_computation.7 | async-start | bytes 3063808 | tf_op jit(solution)/shard_map/all_gather | solution.py:86
  13.1 24.3 %all-to-all-start = ((bf16[8,256,256]{2,1,0:T(8,128)(2,1)}), bf16[8,256,256]{2,1,0:T(8,128)(2,1)S(1)}, u32[]{:S(2)}, u32[]{:S(2)}) async-start(bf16[8,256,256]{2,1,0:T(8,128)(2,1)} %stack.2), calls=%async_computation | async-start | bytes 2097152 | tf_op jit(solution)/shard_map/all_to_all | solution.py:12
  18.5 230.3 %all-gather.5.cloned.1.call-start = ((), (), s32[]{:S(2)}) async-start(), calls=%async_computation.6 | async-start | bytes 3063808 | tf_op jit(solution)/shard_map/all_gather | solution.py:81
  37.3 1.0 copy-start.1
  58.2 151.9 %all-to-all-start.1 = ((bf16[16,2,64,2048]{3,2,1,0:T(8,128)(2,1)}), bf16[16,2,64,2048]{3,2,1,0:T(8,128)(2,1)}, u32[]{:S(2)}, u32[]{:S(2)}) async-start(bf16[16,2,64,2048]{3,2,1,0:T(8,128)(2,1)} %select_select_fusion), calls=%async_computation.1 | async-start | bytes 16777216 | tf_op jit(solution)/shard_map/all_to_all | solution.py:106
  65.3 235.4 %all-gather.11.cloned.1.call-start = ((), (), s32[]{:S(2)}) async-start(), calls=%async_computation.9 | async-start | bytes 3063808 | tf_op jit(solution)/shard_map/all_gather | solution.py:94
  65.8 328.5 %reduce-scatter.3.cloned.1.call-start = ((), (), s32[]{:S(2)}) async-start(), calls=%async_computation.5 | async-start | bytes 18874368 | tf_op jit(solution)/shard_map/reduce_scatter | solution.py:118
  232.8 0.7 copy-start.4
  232.8 0.7 copy-start.5
  232.8 1.6 copy-start.6
  232.9 209.7 %reduce-scatter.5.cloned.1.call-start = ((), (), s32[]{:S(2)}) async-start(), calls=%async_computation.10 | async-start | bytes 2359296 | tf_op jit(solution)/shard_map/reduce_scatter | solution.py:119
  397.5 7.6 %copy-start.2 = (bf16[2048,32]{0,1:T(8,128)(2,1)S(1)}, bf16[2048,32]{0,1:T(8,128)(2,1)}, u32[]{:S(2)}) copy-start(bf16[2048,32]{0,1:T(8,128)(2,1)} %param.16) | copy-start | bytes 393220
  397.6 36.1 %all-to-all-start.2 = ((f32[16,2,64,256]{3,2,1,0:T(8,128)}), f32[16,2,64,256]{3,2,1,0:T(8,128)}, u32[]{:S(2)}, u32[]{:S(2)}) async-start(f32[16,2,64,256]{3,2,1,0:T(8,128)} %copy.54), calls=%async_computation.3 | async-start | bytes 4194304 | tf_op jit(solution)/shard_map/all_to_all | solution.py:121
Sparse Core Ops, SparseCore 0:
  10.5 29.7 all-gather.8
  42.4 128.9 all-gather.6
  173.6 75.2 all-gather.4
  250.8 49.8 all-gather.10
  303.0 91.3 reduce-scatter.2
  396.6 34.4 reduce-scatter.4
